TPU v7x, 32 devices: a whole 2x2x4 slice. The times are simulated.
32 devices in a mesh: slab: 2 (over x), run: 2 (over core), tx: 8 (over z, y).
Axes of the slice: x: 2, y: 2, z: 4, core: 2. Of those that a mesh axis runs over, the one named last changes fastest.
Arguments:
- snapshots: bfloat16 [1024, 128, 512], P(('slab', 'tx'), None, 'run'), parts along dimension 0, may hold values from -60 to 60, as said below
- coefficient: float32 [1024, 128], P(('slab', 'tx')), parts along dimension 0, may hold values from 0.02 to 0.2
- start_first: int32 [512, 128], replicated, may hold values from -4 to 4
- start_merge: int32 [256, 128], replicated, may hold values from -4 to 4
Outputs:
- modes: float32 [1024, 128, 128], P(('slab', 'tx'), None, 'run'), parts along dimension 0
There are 2 independent parts, one for each index of `slab`. A program takes and returns all parts, laid end to end along the dimension named above; an argument that names none is the same for every part. Nothing has to cross between parts.
Inputs may be any that keep to these rules, and one draw needn't show every extreme that they name: `snapshots`: snapshot values are real-valued and bounded.
All inputs are finite; a program needn't handle non-finite values.
Results may differ from a plain program's by a relative error of at most 0.0003.
Values may be sent and summed in bfloat16 or wider, within the bound.
No kernel may reach another device: no remote copies, remote signals or barrier semaphores. Data moves between devices by JAX's collectives and lax.ppermute only.
A program may use at most 128 MiB of HBM per device.

v0:
```python
import jax
import jax.numpy as jnp
from jax import lax
from jax.sharding import PartitionSpec as P

ITERS = 2
highest = lax.Precision.HIGHEST


def padded_2(block, sides, width):
    for axis, dim in sides:
        count = lax.axis_size(axis)
        forward = [(i, i + 1) for i in range(count - 1)]
        backward = [(target, source) for source, target in forward]
        low = lax.ppermute(
            lax.slice_in_dim(block, block.shape[dim] - width, None, axis=dim), axis, forward
        )
        high = lax.ppermute(lax.slice_in_dim(block, 0, width, axis=dim), axis, backward)
        block = jnp.concatenate([low, block, high], axis=dim)
    return block


def partner(block, axis, stride):
    count = lax.axis_size(axis)
    route = []
    for low in range(count):
        high = low | 1 << stride
        if high != low and high < count:
            route += [(low, high), (high, low)]
    return lax.ppermute(block, axis, route)


def fourth_order(values, axis_dim):
    length_kept = values.shape[axis_dim] - 4

    def shifted(offset):
        return lax.slice_in_dim(values, offset, offset + length_kept, axis=axis_dim)

    return (8.0 * (shifted(3) - shifted(1)) - (shifted(4) - shifted(0))) / 12.0


def fluxes(extended, coefficient):
    squared = 0.5 * jnp.square(extended.astype(jnp.float32))
    along_rows = fourth_order(squared, 0)
    padded = jnp.pad(squared[2:-2], ((0, 0), (2, 2), (0, 0)))
    along_cols = fourth_order(padded, 1)
    central = extended[2:-2].astype(jnp.float32)
    return central - coefficient[:, :, None] * (along_rows + along_cols)


def orthonormal(matrix):
    inner_gram = jnp.dot(matrix.T, matrix, precision=highest)
    factor = jnp.linalg.cholesky(inner_gram)
    return jax.scipy.linalg.solve_triangular(factor, matrix.T, lower=True).T


def iterate(gram_matrix, start_int):
    basis_set = orthonormal(start_int.astype(jnp.float32))
    for sweep_index in range(ITERS):
        basis_set = orthonormal(jnp.dot(gram_matrix, basis_set, precision=highest))
    return basis_set


def cross_gram(left_rows, right_rows):
    return lax.dot_general(left_rows, right_rows, (((0,), (0,)), ((), ())), precision=highest)


def on_device(snapshots, coefficient, start_first, start_merge):
    extended = padded_2(snapshots, (("tx", 0),), 2)
    rows_here = snapshots.shape[0] * snapshots.shape[1]
    order_size = snapshots.shape[2]
    modes_count = start_first.shape[1]
    share_count = modes_count // lax.axis_size("run")
    cells_total = rows_here * lax.axis_size("tx")
    member = lax.axis_index("run")
    is_first = member == 0
    own_start = lax.dynamic_slice_in_dim(start_first, member * order_size, order_size, 0)
    own_flux = fluxes(extended, coefficient).reshape(rows_here, order_size)
    own_gram = lax.psum(cross_gram(own_flux, own_flux), "tx") / cells_total
    own_basis = iterate(own_gram, own_start)
    own_modes = jnp.dot(own_flux, own_basis, precision=highest)
    other_modes = partner(own_modes, "run", 0)
    own_block, mixed_block, other_block = lax.psum(
        (
            cross_gram(own_modes, own_modes),
            cross_gram(own_modes, other_modes),
            cross_gram(other_modes, other_modes),
        ),
        "tx",
    )
    own_block = own_block / cells_total
    mixed_block = mixed_block / cells_total
    other_block = other_block / cells_total
    first_block = jnp.where(is_first, own_block, other_block)
    last_block = jnp.where(is_first, other_block, own_block)
    upper_block = jnp.where(is_first, mixed_block, mixed_block.T)
    merge_gram = jnp.concatenate(
        [
            jnp.concatenate([first_block, upper_block], axis=1),
            jnp.concatenate([upper_block.T, last_block], axis=1),
        ],
        axis=0,
    )
    rotation = iterate(merge_gram, start_merge)
    rotation_share = lax.dynamic_slice_in_dim(rotation, member * share_count, share_count, 1)
    top_rows = rotation_share[:modes_count]
    bottom_rows = rotation_share[modes_count:]
    own_rotation = jnp.where(is_first, top_rows, bottom_rows)
    other_rotation = jnp.where(is_first, bottom_rows, top_rows)
    result = jnp.dot(own_modes, own_rotation, precision=highest) + jnp.dot(
        other_modes, other_rotation, precision=highest
    )
    return result.reshape(snapshots.shape[0], snapshots.shape[1], share_count)


def solution(mesh):
    in_specs = (P(("slab", "tx"), None, "run"), P(("slab", "tx"), None), P(), P())
    out_specs = P(("slab", "tx"), None, "run")
    return jax.shard_map(
        on_device, mesh=mesh, in_specs=in_specs, out_specs=out_specs, check_vma=False
    )
```

profile of v0, /device:TPU:0, one launch (start us, length us, event | category | flops | bytes accessed | tf_op | source)
XLA Modules:
  0.0 407.1 jit_solution(16256215032305025658)
XLA Ops:
  6.5 1.0 fusion.71
  7.5 1.3 collective-permute-start.1
  8.8 5.5 %collective-permute-start = (bf16[2,128,256]{2,1,0:T(8,128)(2,1)S(1)}, bf16[2,128,256]{2,1,0:T(8,128)(2,1)S(1)}, u32[]{:S(2)}, u32[]{:S(2)}) collective-permute-start(bf16[2,128,256]{2,1,0:T(8,128)(2,1)S(1)} %get-tuple-element.10), channel_id=1, source_target_pairs={{0,1},{1,2},{2,3},{3,4},{4,5},{5,6},{6,7},{8,9},{9,10},{10,11},{11... | collective-permute-start | bytes 393224 | tf_op jit(solution)/shard_map/ppermute | solution.py:15
  15.1 1.4 fusion.28
  16.6 11.7 %cholesky.104 = f32[128,128]{1,0:T(8,128)S(1)} custom-call(f32[128,128]{1,0:T(8,128)S(1)} %fusion.51), custom_call_target="Cholesky" | custom-call | tf_op jit(solution)/shard_map/jit(cholesky)/cholesky | solution.py:53
  29.0 3.4 multiply_multiply_fusion
  32.4 4.1 %slice.64 = f32[64,128,256]{2,1,0:T(8,128)} slice(f32[68,128,256]{2,1,0:T(8,128)S(1)} %multiply_multiply_fusion), slice={[2:66], [0:128], [0:256]} | slice | bytes 16777216 | tf_op jit(solution)/shard_map/slice | solution.py:45
  36.6 18.5 %fusion.3 = f32[64,128,256]{2,1,0:T(8,128)} fusion(f32[68,128,256]{2,1,0:T(8,128)S(1)} %multiply_multiply_fusion, f32[64,128,256]{2,1,0:T(8,128)} %slice.64, bf16[64,128,256]{2,1,0:T(8,128)(2,1)S(1)} %copy-done, f32[64,128]{1,0:T(8,128)S(1)} %broadcast_multiply_fusion.3), kind=kLoop, calls=%fused_computation.6 | loop fusion | flops 25165824 | bytes 54558720 | tf_op jit(solution)/shard_map/sub | solution.py:48
  55.1 17.7 %convolution_bitcast_fusion = f32[256,256]{1,0:T(8,128)} fusion(f32[64,128,256]{2,1,0:T(8,128)} %fusion.3), kind=kOutput, calls=%fused_computation.12 | convolution fusion | flops 6442450944 | bytes 8650752 | tf_op jit(solution)/shard_map/dot_general | solution.py:65
  73.7 9.8 %custom-call.10 = f32[1,128,128]{1,2,0:T(8,128)S(1)} custom-call(f32[1,128,128]{2,1,0:T(8,128)S(1)} %fusion.34), custom_call_target="InvertDiagBlocksLowerTriangular" | custom-call | tf_op jit(solution)/shard_map/jit(_solve_triangular)/triangular_solve | solution.py:54
  83.8 61.4 %all-reduce.5.cloned.1.call-done = f32[256,256]{1,0:T(8,128)} async-done(((f32[256,256]{1,0:T(8,128)}), f32[256,256]{1,0:T(8,128)}) %all-reduce.5.cloned.1.call-update) | async-done | bytes 262160 | tf_op jit(solution)/shard_map/psum | solution.py:79
  145.3 1.3 fusion.8
  147.1 11.7 %cholesky.115 = f32[128,128]{1,0:T(8,128)S(1)} custom-call(f32[128,128]{1,0:T(8,128)S(1)} %fusion.49), custom_call_target="Cholesky" | custom-call | tf_op jit(solution)/shard_map/jit(cholesky)/cholesky | solution.py:53
  160.2 9.8 %custom-call.11 = f32[1,128,128]{1,2,0:T(8,128)S(1)} custom-call(f32[1,128,128]{2,1,0:T(8,128)S(1)} %fusion.35), custom_call_target="InvertDiagBlocksLowerTriangular" | custom-call | tf_op jit(solution)/shard_map/jit(_solve_triangular)/triangular_solve | solution.py:54
  170.3 1.3 fusion.6
  172.2 11.9 %cholesky.126 = f32[128,128]{1,0:T(8,128)S(1)} custom-call(f32[128,128]{1,0:T(8,128)S(1)} %fusion.47), custom_call_target="Cholesky" | custom-call | tf_op jit(solution)/shard_map/jit(cholesky)/cholesky | solution.py:53
  185.4 9.8 %custom-call.12 = f32[1,128,128]{1,2,0:T(8,128)S(1)} custom-call(f32[1,128,128]{2,1,0:T(8,128)S(1)} %fusion.36), custom_call_target="InvertDiagBlocksLowerTriangular" | custom-call | tf_op jit(solution)/shard_map/jit(_solve_triangular)/triangular_solve | solution.py:54
  195.5 10.8 %fusion.74 = f32[8192,128]{1,0:T(8,128)} fusion(f32[8192,256]{1,0:T(8,128)} %bitcast.109, f32[128,256]{1,0:T(8,128)S(1)} %fusion.18), kind=kOutput, calls=%fused_computation.114 | convolution fusion | flops 3221225472 | bytes 12713984 | tf_op jit(solution)/shard_map/dot_general | solution.py:81
  206.9 11.7 %cholesky.137 = f32[128,128]{1,0:T(8,128)S(1)} custom-call(f32[128,128]{1,0:T(8,128)S(1)} %fusion.45), custom_call_target="Cholesky" | custom-call | tf_op jit(solution)/shard_map/jit(cholesky)/cholesky | solution.py:53
  220.0 9.8 %custom-call.13 = f32[1,128,128]{1,2,0:T(8,128)S(1)} custom-call(f32[1,128,128]{2,1,0:T(8,128)S(1)} %fusion.37), custom_call_target="InvertDiagBlocksLowerTriangular" | custom-call | tf_op jit(solution)/shard_map/jit(_solve_triangular)/triangular_solve | solution.py:54
  229.8 11.0 %fusion.75 = f32[128,128]{1,0:T(8,128)} fusion(f32[8192,128]{1,0:T(8,128)} %fusion.74), kind=kOutput, calls=%fused_computation.115 | convolution fusion | flops 1610612736 | bytes 4259840 | tf_op jit(solution)/shard_map/dot_general | solution.py:65
  240.8 10.8 %fusion.76 = f32[128,128]{0,1:T(8,128)} fusion(f32[8192,128]{1,0:T(8,128)} %collective-permute-done.2), kind=kOutput, calls=%fused_computation.116 | convolution fusion | flops 1610612736 | bytes 4259840 | tf_op jit(solution)/shard_map/dot_general | solution.py:65
  251.6 11.0 %fusion.77 = f32[128,128]{0,1:T(8,128)} fusion(f32[8192,128]{1,0:T(8,128)} %fusion.74, f32[8192,128]{1,0:T(8,128)} %collective-permute-done.2), kind=kOutput, calls=%fused_computation.117 | convolution fusion | flops 1610612736 | bytes 8454144 | tf_op jit(solution)/shard_map/dot_general | solution.py:65
  263.0 70.1 %all-reduce.7.cloned.1.call-done = (f32[128,128]{0,1:T(8,128)}, f32[128,128]{1,0:T(8,128)}, f32[128,128]{0,1:T(8,128)}) async-done(((f32[128,128]{0,1:T(8,128)}, f32[128,128]{1,0:T(8,128)}, f32[128,128]{0,1:T(8,128)}), (f32[128,128]{0,1:T(8,128)}, f32[128,128]{1,0:T(8,128)}, f32[128,128]{0,1:T(8,128)})) %all-reduce.7.cloned.1.call-update) | async-done | bytes 196624 | tf_op jit(solution)/shard_map/psum | solution.py:83
  334.0 0.9 bitcast_select_fusion
  337.9 11.7 %cholesky.148 = f32[128,128]{1,0:T(8,128)S(1)} custom-call(f32[128,128]{1,0:T(8,128)S(1)} %fusion.43), custom_call_target="Cholesky" | custom-call | tf_op jit(solution)/shard_map/jit(cholesky)/cholesky | solution.py:53
  350.9 9.8 %custom-call.14 = f32[1,128,128]{1,2,0:T(8,128)S(1)} custom-call(f32[1,128,128]{2,1,0:T(8,128)S(1)} %fusion.38), custom_call_target="InvertDiagBlocksLowerTriangular" | custom-call | tf_op jit(solution)/shard_map/jit(_solve_triangular)/triangular_solve | solution.py:54
  361.9 11.9 %cholesky.159 = f32[128,128]{1,0:T(8,128)S(1)} custom-call(f32[128,128]{1,0:T(8,128)S(1)} %fusion.41), custom_call_target="Cholesky" | custom-call | tf_op jit(solution)/shard_map/jit(cholesky)/cholesky | solution.py:53
  375.2 9.8 %custom-call.15 = f32[1,128,128]{1,2,0:T(8,128)S(1)} custom-call(f32[1,128,128]{2,1,0:T(8,128)S(1)} %fusion.39), custom_call_target="InvertDiagBlocksLowerTriangular" | custom-call | tf_op jit(solution)/shard_map/jit(_solve_triangular)/triangular_solve | solution.py:54
  385.4 6.4 %fusion.57 = f32[8192,64]{0,1:T(8,128)S(1)} fusion(f32[8192,128]{1,0:T(8,128)} %fusion.74, f32[256,64]{0,1:T(8,128)S(1)} %dynamic-slice_bitcast_fusion, pred[]{:T(512)S(6)} %eq.3), kind=kOutput, calls=%fused_computation.86 | convolution fusion | flops 805314560 | bytes 6356993 | tf_op jit(solution)/shard_map/dot_general | solution.py:110
  391.8 6.4 %fusion.5 = f32[8,64,8,128]{3,2,1,0:T(8,128)S(1)} fusion(f32[8192,64]{0,1:T(8,128)S(1)} %fusion.57, f32[8192,128]{1,0:T(8,128)} %collective-permute-done.2, f32[256,64]{0,1:T(8,128)S(1)} %dynamic-slice_bitcast_fusion, pred[]{:T(512)S(6)} %eq.3), kind=kOutput, calls=%fused_computation.11 | convolution fusion | flops 805838848 | bytes 8454145 | tf_op jit(solution)/shard_map/dot_general | solution.py:110
  398.2 1.6 copy.28
  (67 shorter events, 17.2 us)
Async XLA Ops:
  6.5 138.7 %all-reduce.5.cloned.1.call-start = ((), (), s32[]{:S(2)}) async-start(), calls=%async_computation | async-start | bytes 524288 | tf_op jit(solution)/shard_map/psum | solution.py:79
  7.5 21.5 %collective-permute-start.1 = (bf16[2,128,256]{2,1,0:T(8,128)(2,1)S(1)}, bf16[2,128,256]{2,1,0:T(8,128)(2,1)S(1)}, u32[]{:S(2)}, u32[]{:S(2)}) collective-permute-start(bf16[2,128,256]{2,1,0:T(8,128)(2,1)S(1)} %get-tuple-element.11), channel_id=1, source_target_pairs={{1,0},{2,1},{3,2},{4,3},{5,4},{6,5},{7,6},{9,8},{10,9},{11,10},{12... | collective-permute-start | bytes 393224 | tf_op jit(solution)/shard_map/ppermute | solution.py:18
  8.8 20.2 %collective-permute-start = (bf16[2,128,256]{2,1,0:T(8,128)(2,1)S(1)}, bf16[2,128,256]{2,1,0:T(8,128)(2,1)S(1)}, u32[]{:S(2)}, u32[]{:S(2)}) collective-permute-start(bf16[2,128,256]{2,1,0:T(8,128)(2,1)S(1)} %get-tuple-element.10), channel_id=1, source_target_pairs={{0,1},{1,2},{2,3},{3,4},{4,5},{5,6},{6,7},{8,9},{9,10},{10,11},{11... | collective-permute-start | bytes 393224 | tf_op jit(solution)/shard_map/ppermute | solution.py:15
  32.4 4.2 %copy-start = (bf16[64,128,256]{2,1,0:T(8,128)(2,1)S(1)}, bf16[64,128,256]{2,1,0:T(8,128)(2,1)}, u32[]{:S(2)}) copy-start(bf16[64,128,256]{2,1,0:T(8,128)(2,1)} %param.7) | copy-start | bytes 12582916
  55.1 28.4 %copy-start.2 = (s32[512,128]{1,0:T(8,128)S(1)}, s32[512,128]{1,0:T(8,128)}, u32[]{:S(2)}) copy-start(s32[512,128]{1,0:T(8,128)} %param.9) | copy-start | bytes 786436
  72.9 260.1 %all-reduce.7.cloned.1.call-start = ((), (), s32[]{:S(2)}) async-start(), calls=%async_computation.1 | async-start | bytes 393216 | tf_op jit(solution)/shard_map/psum | solution.py:83
  195.5 10.9 %copy-start.1 = (s32[256,128]{1,0:T(8,128)S(1)}, s32[256,128]{1,0:T(8,128)}, u32[]{:S(2)}) copy-start(s32[256,128]{1,0:T(8,128)} %param.10) | copy-start | bytes 393220
  206.3 34.5 %collective-permute-start.2 = (f32[8192,128]{1,0:T(8,128)}, f32[8192,128]{1,0:T(8,128)}, u32[]{:S(2)}, u32[]{:S(2)}) collective-permute-start(f32[8192,128]{1,0:T(8,128)} %fusion.74), channel_id=1, source_target_pairs={{0,8},{8,0},{1,9},{9,1},{2,10},{10,2},{3,11},{11,3},{4,12},{12,4},... | collective-permute-start | bytes 12582920 | tf_op jit(solution)/shard_map/ppermute | solution.py:30
Sparse Core Ops, SparseCore 0:
  73.0 72.2 all-reduce.4
  262.8 70.2 all-reduce.6
where the time goes:
time: 411 us; the launch traced here: 407 us
  other arithmetic  164 us (40%)
  waiting for transfers between devices  132 us (32%)
  matrix products  82.7 us (20%)
  between operations  14.3 us (3%)
  local copies, waits for them, and re-layouts  7.74 us (2%)
  starting transfers between devices  7.09 us (2%)
    another operation x18, other arithmetic, orthonormal(): factor = jnp.linalg.cholesky(inner_gram)  74.7 us
    psum x1, waiting for transfers between devices, on_device(): lax.psum((cross_gram(own_modes, own_modes), cross_gram(own_modes, other_m...  70.1 us
    another operation x12, other arithmetic, orthonormal(): return jax.scipy.linalg.solve_triangular(factor, matrix.T, lower=True).T  62.7 us
    psum x1, waiting for transfers between devices, on_device(): own_gram = lax.psum(cross_gram(own_flux, own_flux), 'tx') / cells_total  61.4 us
    dot_general x4, matrix products, cross_gram(): lax.dot_general(left_rows, right_rows, (((0,), (0,)), ((), ())), precisio...  50.6 us
    sub x1, other arithmetic, fluxes(): return central - coefficient[:, :, None] * (along_rows + along_cols)  18.5 us
    dot_general x1, matrix products, on_device(): own_modes = jnp.dot(own_flux, own_basis, precision=highest)  10.8 us
  transfers between devices with their start and end apart: 5, of which 2 were waited for; matrix products, arithmetic and copies ran while one was open for 15% of the time, Pallas kernels for 0%

commit v1 on v0

--- a/solution.py
+++ b/solution.py
@@ -5,6 +5,10 @@
 
 ITERS = 2
 highest = lax.Precision.HIGHEST
+
+
+def mix_unit_in(my_tile):
+    return jax.lax.all_gather(my_tile, "tx").sum(axis=0)
 
 
 def padded_2(block, sides, width):
@@ -76,7 +80,7 @@
     is_first = member == 0
     own_start = lax.dynamic_slice_in_dim(start_first, member * order_size, order_size, 0)
     own_flux = fluxes(extended, coefficient).reshape(rows_here, order_size)
-    own_gram = lax.psum(cross_gram(own_flux, own_flux), "tx") / cells_total
+    own_gram = mix_unit_in(cross_gram(own_flux, own_flux)) / cells_total
     own_basis = iterate(own_gram, own_start)
     own_modes = jnp.dot(own_flux, own_basis, precision=highest)
     other_modes = partner(own_modes, "run", 0)

time: 411 us -> 382 us (0.929)
  waiting for transfers between devices: 132 us -> 99.8 us
    psum x1 -> x0, waiting for transfers between devices: 61.4 us -> none  [on_device(): own_gram = lax.psum(cross_gram(own_flux, own_flux), 'tx') / cells_total]
    all_gather x0 -> x1, waiting for transfers between devices: none -> 26.8 us  [mix_unit_in(): return jax.lax.all_gather(my_tile, 'tx').sum(axis=0)]
  transfers between devices with their start and end apart: 5 -> 5, of which waited for: 2 -> 4; matrix products, arithmetic and copies ran while one was open for 15% -> 16% of each run, Pallas kernels for 0% -> 0%
where the time goes in v1:
time: 382 us; the launch traced here: 374 us
  other arithmetic  165 us (43%)
  waiting for transfers between devices  99.8 us (26%)
  matrix products  79.9 us (21%)
  between operations  14.3 us (4%)
  local copies, waits for them, and re-layouts  7.74 us (2%)
  starting transfers between devices  7.38 us (2%)
    another operation x18, other arithmetic, orthonormal(): factor = jnp.linalg.cholesky(inner_gram)  74.6 us
    psum x1, waiting for transfers between devices, on_device(): lax.psum((cross_gram(own_modes, own_modes), cross_gram(own_modes, other_m...  69.3 us
    another operation x12, other arithmetic, orthonormal(): return jax.scipy.linalg.solve_triangular(factor, matrix.T, lower=True).T  63 us
    dot_general x4, matrix products, cross_gram(): lax.dot_general(left_rows, right_rows, (((0,), (0,)), ((), ())), precisio...  50.6 us
    all_gather x1, waiting for transfers between devices, mix_unit_in(): return jax.lax.all_gather(my_tile, 'tx').sum(axis=0)  26.8 us
    sub x1, other arithmetic, fluxes(): return central - coefficient[:, :, None] * (along_rows + along_cols)  18.5 us
    dot_general x1, matrix products, on_device(): own_modes = jnp.dot(own_flux, own_basis, precision=highest)  10.8 us
  transfers between devices with their start and end apart: 5, of which 4 were waited for; matrix products, arithmetic and copies ran while one was open for 16% of the time, Pallas kernels for 0%

profile of v1, /device:TPU:0, one launch (start us, length us, event | category | flops | bytes accessed | tf_op | source)
XLA Modules:
  0.0 374.3 jit_solution(873098190737890891)
XLA Ops:
  6.5 1.0 fusion.71
  7.5 1.3 collective-permute-start.1
  8.8 5.5 %collective-permute-start = (bf16[2,128,256]{2,1,0:T(8,128)(2,1)S(1)}, bf16[2,128,256]{2,1,0:T(8,128)(2,1)S(1)}, u32[]{:S(2)}, u32[]{:S(2)}) collective-permute-start(bf16[2,128,256]{2,1,0:T(8,128)(2,1)S(1)} %get-tuple-element.10), channel_id=1, source_target_pairs={{0,1},{1,2},{2,3},{3,4},{4,5},{5,6},{6,7},{8,9},{9,10},{10,11},{11... | collective-permute-start | bytes 393224 | tf_op jit(solution)/shard_map/ppermute | solution.py:19
  15.9 3.0 collective-permute-done
  18.8 3.0 multiply_multiply_fusion
  21.8 4.1 %slice.64 = f32[64,128,256]{2,1,0:T(8,128)} slice(f32[68,128,256]{2,1,0:T(8,128)S(1)} %multiply_multiply_fusion), slice={[2:66], [0:128], [0:256]} | slice | bytes 16777216 | tf_op jit(solution)/shard_map/slice | solution.py:49
  26.0 18.5 %fusion.3 = f32[64,128,256]{2,1,0:T(8,128)} fusion(f32[68,128,256]{2,1,0:T(8,128)S(1)} %multiply_multiply_fusion, f32[64,128,256]{2,1,0:T(8,128)} %slice.64, bf16[64,128,256]{2,1,0:T(8,128)(2,1)S(1)} %copy-done, f32[64,128]{1,0:T(8,128)S(1)} %broadcast_multiply_fusion.3), kind=kLoop, calls=%fused_computation.6 | loop fusion | flops 25165824 | bytes 54558720 | tf_op jit(solution)/shard_map/sub | solution.py:52
  44.5 17.7 %convolution_bitcast_fusion = f32[256,256]{1,0:T(8,128)} fusion(f32[64,128,256]{2,1,0:T(8,128)} %fusion.3), kind=kOutput, calls=%fused_computation.12 | convolution fusion | flops 6442450944 | bytes 8650752 | tf_op jit(solution)/shard_map/dot_general | solution.py:69
  63.4 11.7 %cholesky.104 = f32[128,128]{1,0:T(8,128)S(1)} custom-call(f32[128,128]{1,0:T(8,128)S(1)} %fusion.51), custom_call_target="Cholesky" | custom-call | tf_op jit(solution)/shard_map/jit(cholesky)/cholesky | solution.py:57
  76.5 9.8 %custom-call.10 = f32[1,128,128]{1,2,0:T(8,128)S(1)} custom-call(f32[1,128,128]{2,1,0:T(8,128)S(1)} %fusion.34), custom_call_target="InvertDiagBlocksLowerTriangular" | custom-call | tf_op jit(solution)/shard_map/jit(_solve_triangular)/triangular_solve | solution.py:58
  86.6 26.8 %all-gather.3.cloned.1.call-done = f32[2048,256]{1,0:T(8,128)} async-done(((f32[256,256]{1,0:T(8,128)}), f32[2048,256]{1,0:T(8,128)}) %all-gather.3.cloned.1.call-update) | async-done | bytes 2097168 | tf_op jit(solution)/shard_map/all_gather | solution.py:11
  113.4 1.8 reduce_sum.9
  116.1 11.7 %cholesky.115 = f32[128,128]{1,0:T(8,128)S(1)} custom-call(f32[128,128]{1,0:T(8,128)S(1)} %fusion.49), custom_call_target="Cholesky" | custom-call | tf_op jit(solution)/shard_map/jit(cholesky)/cholesky | solution.py:57
  129.1 10.0 %custom-call.11 = f32[1,128,128]{1,2,0:T(8,128)S(1)} custom-call(f32[1,128,128]{2,1,0:T(8,128)S(1)} %fusion.35), custom_call_target="InvertDiagBlocksLowerTriangular" | custom-call | tf_op jit(solution)/shard_map/jit(_solve_triangular)/triangular_solve | solution.py:58
  140.3 11.7 %cholesky.126 = f32[128,128]{1,0:T(8,128)S(1)} custom-call(f32[128,128]{1,0:T(8,128)S(1)} %fusion.47), custom_call_target="Cholesky" | custom-call | tf_op jit(solution)/shard_map/jit(cholesky)/cholesky | solution.py:57
  153.3 9.8 %custom-call.12 = f32[1,128,128]{1,2,0:T(8,128)S(1)} custom-call(f32[1,128,128]{2,1,0:T(8,128)S(1)} %fusion.36), custom_call_target="InvertDiagBlocksLowerTriangular" | custom-call | tf_op jit(solution)/shard_map/jit(_solve_triangular)/triangular_solve | solution.py:58
  163.5 10.8 %fusion.74 = f32[8192,128]{1,0:T(8,128)} fusion(f32[8192,256]{1,0:T(8,128)} %bitcast.110, f32[128,256]{1,0:T(8,128)S(1)} %fusion.18), kind=kOutput, calls=%fused_computation.114 | convolution fusion | flops 3221225472 | bytes 12713984 | tf_op jit(solution)/shard_map/dot_general | solution.py:85
  174.9 11.7 %cholesky.137 = f32[128,128]{1,0:T(8,128)S(1)} custom-call(f32[128,128]{1,0:T(8,128)S(1)} %fusion.45), custom_call_target="Cholesky" | custom-call | tf_op jit(solution)/shard_map/jit(cholesky)/cholesky | solution.py:57
  187.9 9.8 %custom-call.13 = f32[1,128,128]{1,2,0:T(8,128)S(1)} custom-call(f32[1,128,128]{2,1,0:T(8,128)S(1)} %fusion.37), custom_call_target="InvertDiagBlocksLowerTriangular" | custom-call | tf_op jit(solution)/shard_map/jit(_solve_triangular)/triangular_solve | solution.py:58
  197.7 11.0 %fusion.75 = f32[128,128]{1,0:T(8,128)} fusion(f32[8192,128]{1,0:T(8,128)} %fusion.74), kind=kOutput, calls=%fused_computation.115 | convolution fusion | flops 1610612736 | bytes 4259840 | tf_op jit(solution)/shard_map/dot_general | solution.py:69
  208.7 10.8 %fusion.76 = f32[128,128]{0,1:T(8,128)} fusion(f32[8192,128]{1,0:T(8,128)} %collective-permute-done.2), kind=kOutput, calls=%fused_computation.116 | convolution fusion | flops 1610612736 | bytes 4259840 | tf_op jit(solution)/shard_map/dot_general | solution.py:69
  219.5 11.0 %fusion.77 = f32[128,128]{0,1:T(8,128)} fusion(f32[8192,128]{1,0:T(8,128)} %fusion.74, f32[8192,128]{1,0:T(8,128)} %collective-permute-done.2), kind=kOutput, calls=%fused_computation.117 | convolution fusion | flops 1610612736 | bytes 8454144 | tf_op jit(solution)/shard_map/dot_general | solution.py:69
  230.9 69.3 %all-reduce.4.cloned.1.call-done = (f32[128,128]{0,1:T(8,128)}, f32[128,128]{1,0:T(8,128)}, f32[128,128]{0,1:T(8,128)}) async-done(((f32[128,128]{0,1:T(8,128)}, f32[128,128]{1,0:T(8,128)}, f32[128,128]{0,1:T(8,128)}), (f32[128,128]{0,1:T(8,128)}, f32[128,128]{1,0:T(8,128)}, f32[128,128]{0,1:T(8,128)})) %all-reduce.4.cloned.1.call-update) | async-done | bytes 196624 | tf_op jit(solution)/shard_map/psum | solution.py:87
  301.1 0.9 bitcast_select_fusion
  302.1 0.9 broadcast_select_fusion.1
  305.0 11.7 %cholesky.148 = f32[128,128]{1,0:T(8,128)S(1)} custom-call(f32[128,128]{1,0:T(8,128)S(1)} %fusion.43), custom_call_target="Cholesky" | custom-call | tf_op jit(solution)/shard_map/jit(cholesky)/cholesky | solution.py:57
  318.1 9.8 %custom-call.14 = f32[1,128,128]{1,2,0:T(8,128)S(1)} custom-call(f32[1,128,128]{2,1,0:T(8,128)S(1)} %fusion.38), custom_call_target="InvertDiagBlocksLowerTriangular" | custom-call | tf_op jit(solution)/shard_map/jit(_solve_triangular)/triangular_solve | solution.py:58
  329.1 11.9 %cholesky.159 = f32[128,128]{1,0:T(8,128)S(1)} custom-call(f32[128,128]{1,0:T(8,128)S(1)} %fusion.41), custom_call_target="Cholesky" | custom-call | tf_op jit(solution)/shard_map/jit(cholesky)/cholesky | solution.py:57
  342.4 9.8 %custom-call.15 = f32[1,128,128]{1,2,0:T(8,128)S(1)} custom-call(f32[1,128,128]{2,1,0:T(8,128)S(1)} %fusion.39), custom_call_target="InvertDiagBlocksLowerTriangular" | custom-call | tf_op jit(solution)/shard_map/jit(_solve_triangular)/triangular_solve | solution.py:58
  352.5 6.4 %fusion.57 = f32[8192,64]{0,1:T(8,128)S(1)} fusion(f32[8192,128]{1,0:T(8,128)} %fusion.74, f32[256,64]{0,1:T(8,128)S(1)} %dynamic-slice_bitcast_fusion, pred[]{:T(512)S(6)} %eq.3), kind=kOutput, calls=%fused_computation.86 | convolution fusion | flops 805314560 | bytes 6356993 | tf_op jit(solution)/shard_map/dot_general | solution.py:114
  359.0 6.4 %fusion.5 = f32[8,64,8,128]{3,2,1,0:T(8,128)S(1)} fusion(f32[8192,64]{0,1:T(8,128)S(1)} %fusion.57, f32[8192,128]{1,0:T(8,128)} %collective-permute-done.2, f32[256,64]{0,1:T(8,128)S(1)} %dynamic-slice_bitcast_fusion, pred[]{:T(512)S(6)} %eq.3), kind=kOutput, calls=%fused_computation.11 | convolution fusion | flops 805838848 | bytes 8454145 | tf_op jit(solution)/shard_map/dot_general | solution.py:114
  365.4 1.6 copy.28
  (68 shorter events, 18.8 us)
Async XLA Ops:
  6.5 106.9 %all-gather.3.cloned.1.call-start = ((), (), s32[]{:S(2)}) async-start(), calls=%async_computation | async-start | bytes 2359296 | tf_op jit(solution)/shard_map/all_gather | solution.py:11
  7.5 8.4 %collective-permute-start.1 = (bf16[2,128,256]{2,1,0:T(8,128)(2,1)S(1)}, bf16[2,128,256]{2,1,0:T(8,128)(2,1)S(1)}, u32[]{:S(2)}, u32[]{:S(2)}) collective-permute-start(bf16[2,128,256]{2,1,0:T(8,128)(2,1)S(1)} %get-tuple-element.11), channel_id=1, source_target_pairs={{1,0},{2,1},{3,2},{4,3},{5,4},{6,5},{7,6},{9,8},{10,9},{11,10},{12... | collective-permute-start | bytes 393224 | tf_op jit(solution)/shard_map/ppermute | solution.py:22
  8.8 10.0 %collective-permute-start = (bf16[2,128,256]{2,1,0:T(8,128)(2,1)S(1)}, bf16[2,128,256]{2,1,0:T(8,128)(2,1)S(1)}, u32[]{:S(2)}, u32[]{:S(2)}) collective-permute-start(bf16[2,128,256]{2,1,0:T(8,128)(2,1)S(1)} %get-tuple-element.10), channel_id=1, source_target_pairs={{0,1},{1,2},{2,3},{3,4},{4,5},{5,6},{6,7},{8,9},{9,10},{10,11},{11... | collective-permute-start | bytes 393224 | tf_op jit(solution)/shard_map/ppermute | solution.py:19
  21.8 4.2 %copy-start = (bf16[64,128,256]{2,1,0:T(8,128)(2,1)S(1)}, bf16[64,128,256]{2,1,0:T(8,128)(2,1)}, u32[]{:S(2)}) copy-start(bf16[64,128,256]{2,1,0:T(8,128)(2,1)} %param.7) | copy-start | bytes 12582916
  44.5 18.3 %copy-start.2 = (s32[512,128]{1,0:T(8,128)S(1)}, s32[512,128]{1,0:T(8,128)}, u32[]{:S(2)}) copy-start(s32[512,128]{1,0:T(8,128)} %param.9) | copy-start | bytes 786436
  62.3 237.9 %all-reduce.4.cloned.1.call-start = ((), (), s32[]{:S(2)}) async-start(), calls=%async_computation.1 | async-start | bytes 393216 | tf_op jit(solution)/shard_map/psum | solution.py:87
  163.5 10.9 %copy-start.1 = (s32[256,128]{1,0:T(8,128)S(1)}, s32[256,128]{1,0:T(8,128)}, u32[]{:S(2)}) copy-start(s32[256,128]{1,0:T(8,128)} %param.10) | copy-start | bytes 393220
  174.3 34.5 %collective-permute-start.2 = (f32[8192,128]{1,0:T(8,128)}, f32[8192,128]{1,0:T(8,128)}, u32[]{:S(2)}, u32[]{:S(2)}) collective-permute-start(f32[8192,128]{1,0:T(8,128)} %fusion.74), channel_id=1, source_target_pairs={{0,8},{8,0},{1,9},{9,1},{2,10},{10,2},{3,11},{11,3},{4,12},{12,4},... | collective-permute-start | bytes 12582920 | tf_op jit(solution)/shard_map/ppermute | solution.py:34
Sparse Core Ops, SparseCore 0:
  62.4 50.9 all-gather.2
  230.7 69.4 all-reduce.3
